TPU v7x, 128 devices: a whole 4x4x4 slice. The times are simulated.
128 devices in a mesh: pool: 4 (over x_hi, core), grp: 4 (over y), tp: 8 (over z, x_lo).
Axes of the slice: x: 4 (x_hi: 2, x_lo: 2; x = x_hi * 2 + x_lo), y: 4, z: 4, core: 2. Of those that a mesh axis runs over, the one named last changes fastest.
Arguments:
- hidden: bfloat16 [1024, 8192], P('pool', 'grp'), may hold values from -6 to 6
- attn_gain: float32 [8192], P('grp'), may hold values from 0.25 to 1.75
- w_query: bfloat16 [8192, 8192], P('grp', 'tp'), may hold values from -0.0625 to 0.0625
- w_key: bfloat16 [8192, 1024], P('grp', 'tp'), may hold values from -1 to 1
- w_value: bfloat16 [8192, 1024], P('grp', 'tp'), may hold values from -0.0625 to 0.0625
- w_out: bfloat16 [8192, 8192], P('tp', 'grp'), may hold values from -0.0625 to 0.0625
- prefix_keys: bfloat16 [8, 16384, 1024], P('pool', 'grp', 'tp'), may hold values from -300 to 300
- prefix_values: bfloat16 [8, 16384, 1024], P('pool', 'grp', 'tp'), may hold values from -6 to 6
- suffix_keys: bfloat16 [1024, 256, 1024], P('pool', 'grp', 'tp'), may hold values from -300 to 300
- suffix_values: bfloat16 [1024, 256, 1024], P('pool', 'grp', 'tp'), may hold values from -6 to 6
- prefix_ids: int32 [1024], P('pool'), may hold values from 0 to 7, as said below
- suffix_lens: int32 [1024], P('pool'), may hold values from 1 to 256, as said below
- ffn_gain: float32 [8192], P('grp'), may hold values from 0.25 to 1.75
- w_gate: bfloat16 [8192, 14336], P('grp', ('pool', 'tp')), may hold values from -0.0625 to 0.0625
- w_up: bfloat16 [8192, 14336], P('grp', ('pool', 'tp')), may hold values from -0.0625 to 0.0625
- w_down: bfloat16 [14336, 8192], P(('pool', 'tp'), 'grp'), may hold values from -0.046875 to 0.046875
Outputs:
- result: bfloat16 [1024, 8192], P(('pool', 'tp'), 'grp')
Inputs may be any that keep to these rules, and one draw needn't show every extreme that they name: `prefix_ids`: within rows p * 256 to (p + 1) * 256 - 1, each of the prefixes p * 2 to (p + 1) * 2 - 1 is named by exactly 128 streams, and no other prefix is named. `suffix_lens`: each block of 256 streams holds a stream of length 256 and one of length 1.
All inputs are finite; a program needn't handle non-finite values.
Results may differ from a plain program's by a relative error of at most 0.015.
Values may be sent and summed in bfloat16 or wider, within the bound.
No kernel may reach another device: no remote copies, remote signals or barrier semaphores. Data moves between devices by JAX's collectives and lax.ppermute only.
A program may use at most 192 MiB of HBM per device.

v0:
```python
import math
import jax
import jax.numpy as jnp
from jax import lax
from jax.sharding import PartitionSpec as P

D = 8192
HD = 128
epsilon = 1e-05


def joined(array, axis, combine):
    everything = jax.tree.map(lambda part: lax.all_gather(part, axis), array)
    first = jax.tree.map(lambda part: part[0], everything)

    def lap(k, so_far):
        return combine(so_far, jax.tree.map(lambda part: part[k], everything))

    return lax.fori_loop(1, lax.axis_size(axis), lap, first)


def combine_parts(earlier, later):
    peak_one, total_one, numer_one = earlier
    peak_two, total_two, numer_two = later
    peak = jnp.maximum(peak_one, peak_two)
    scale_one = jnp.exp(peak_one - peak)
    scale_two = jnp.exp(peak_two - peak)
    total = total_one * scale_one + total_two * scale_two
    numer = numer_one * scale_one[..., None] + numer_two * scale_two[..., None]
    return (peak, total, numer)


def body(
    hidden,
    attn_gain,
    w_query,
    w_key,
    w_value,
    w_out,
    prefix_keys,
    prefix_values,
    suffix_keys,
    suffix_values,
    prefix_ids,
    suffix_lens,
    ffn_gain,
    w_gate,
    w_up,
    w_down,
):
    stream_count = hidden.shape[0]
    hidden_float = hidden.astype(jnp.float32)
    squares = lax.psum(jnp.sum(hidden_float * hidden_float, axis=1), "grp")
    inverse = lax.rsqrt(squares / D + epsilon)
    normed = (hidden_float * inverse[:, None] * attn_gain).astype(jnp.bfloat16)
    part_query = jnp.dot(normed, w_query, preferred_element_type=jnp.float32)
    part_key = jnp.dot(normed, w_key, preferred_element_type=jnp.float32)
    part_value = jnp.dot(normed, w_value, preferred_element_type=jnp.float32)
    query, key_new, value_new = lax.psum((part_query, part_key, part_value), "grp")
    query = query.astype(jnp.bfloat16)
    key_new = key_new.astype(jnp.bfloat16)
    value_new = value_new.astype(jnp.bfloat16)
    kv_local = w_key.shape[1] // HD
    q_local = w_query.shape[1] // HD
    groups = q_local // kv_local
    prefix_local = prefix_keys.shape[0]
    pre_length = prefix_keys.shape[1]
    suf_length = suffix_keys.shape[1]
    factor = 1.0 / math.sqrt(HD)
    heads = query.reshape(stream_count, kv_local, groups, HD)
    pre_key = prefix_keys.reshape(prefix_local, pre_length, kv_local, HD)
    pre_value = prefix_values.reshape(prefix_local, pre_length, kv_local, HD)
    suf_key = suffix_keys.reshape(stream_count, suf_length, kv_local, HD)
    suf_value = suffix_values.reshape(stream_count, suf_length, kv_local, HD)
    local_prefix = prefix_ids - lax.axis_index("pool") * prefix_local
    per_group = stream_count // prefix_local
    one_hot = (local_prefix[:, None] == jnp.arange(prefix_local, dtype=jnp.int32)[None, :]).astype(
        jnp.int32
    )
    rank_within = jnp.sum(jnp.cumsum(one_hot, axis=0) * one_hot, axis=1) - 1
    target = local_prefix * per_group + rank_within
    group_order = (
        jnp.zeros((stream_count,), jnp.int32)
        .at[target]
        .set(jnp.arange(stream_count, dtype=jnp.int32))
    )
    grouped = heads[group_order].reshape(prefix_local, per_group, kv_local, groups, HD)
    pre_scores = (
        jnp.einsum("pskgd,pjkd->pskgj", grouped, pre_key, preferred_element_type=jnp.float32)
        * factor
    )
    pre_peak = pre_scores.max(axis=4).reshape(stream_count, kv_local, groups)[target]
    positions = lax.axis_index("grp") * suf_length + jnp.arange(suf_length, dtype=jnp.int32)
    valid = (positions[None, :] < suffix_lens[:, None])[:, None, None, :]
    suf_scores = (
        jnp.einsum("skgd,sjkd->skgj", heads, suf_key, preferred_element_type=jnp.float32) * factor
    )
    suf_scores = jnp.where(valid, suf_scores, -1e30)
    peak = jnp.maximum(pre_peak, suf_scores.max(axis=3))
    peak_grouped = peak[group_order].reshape(prefix_local, per_group, kv_local, groups)
    pre_weights = jnp.exp(pre_scores - peak_grouped[..., None]).astype(jnp.bfloat16)
    pre_total = (
        pre_weights.astype(jnp.float32).sum(axis=4).reshape(stream_count, kv_local, groups)[target]
    )
    pre_numer = jnp.einsum(
        "pskgj,pjkd->pskgd", pre_weights, pre_value, preferred_element_type=jnp.float32
    )
    pre_numer = pre_numer.reshape(stream_count, kv_local, groups, HD)[target]
    suf_weights = jnp.where(valid, jnp.exp(suf_scores - peak[:, :, :, None]), 0.0).astype(
        jnp.bfloat16
    )
    total = pre_total + suf_weights.astype(jnp.float32).sum(axis=3)
    numer = pre_numer + jnp.einsum(
        "skgj,sjkd->skgd", suf_weights, suf_value, preferred_element_type=jnp.float32
    )
    peak, total, numer = joined((peak, total, numer), "grp", combine_parts)
    own_score = (
        jnp.einsum(
            "skgd,skd->skg",
            heads,
            key_new.reshape(stream_count, kv_local, HD),
            preferred_element_type=jnp.float32,
        )
        * factor
    )
    new_peak = jnp.maximum(peak, own_score)
    rescale = jnp.exp(peak - new_peak)
    own_weight = jnp.exp(own_score - new_peak).astype(jnp.bfloat16).astype(jnp.float32)
    total = total * rescale + own_weight
    own_value = value_new.reshape(stream_count, kv_local, 1, HD).astype(jnp.float32)
    numer = numer * rescale[..., None] + own_weight[..., None] * own_value
    attended = (numer / total[..., None]).reshape(stream_count, q_local * HD).astype(jnp.bfloat16)
    partial_out = jnp.dot(attended, w_out, preferred_element_type=jnp.float32)
    share = stream_count // lax.axis_size("tp")
    tp_start = lax.axis_index("tp") * share
    summed = lax.psum(partial_out, "tp")
    summed = lax.dynamic_slice_in_dim(summed, tp_start, share, 0)
    own_hidden = lax.dynamic_slice_in_dim(hidden_float, tp_start, share, 0)
    middle = (own_hidden + summed).astype(jnp.bfloat16)
    gathered = lax.all_gather(middle, ("pool", "tp"), axis=0, tiled=True)
    gathered_float = gathered.astype(jnp.float32)
    ffn_squares = lax.psum(jnp.sum(gathered_float * gathered_float, axis=1), "grp")
    ffn_inverse = lax.rsqrt(ffn_squares / D + epsilon)
    normed_ffn = (gathered_float * ffn_inverse[:, None] * ffn_gain).astype(jnp.bfloat16)
    part_gate = jnp.dot(normed_ffn, w_gate, preferred_element_type=jnp.float32)
    part_upward = jnp.dot(normed_ffn, w_up, preferred_element_type=jnp.float32)
    gate, upward = lax.psum((part_gate, part_upward), "grp")
    act = (jax.nn.silu(gate) * upward).astype(jnp.bfloat16)
    returned = lax.psum_scatter(
        jnp.dot(act, w_down, preferred_element_type=jnp.float32),
        ("pool", "tp"),
        scatter_dimension=0,
        tiled=True,
    )
    return (middle.astype(jnp.float32) + returned).astype(jnp.bfloat16)


def solution(mesh):
    return jax.shard_map(
        body,
        mesh=mesh,
        in_specs=(
            P("pool", "grp"),
            P("grp"),
            P("grp", "tp"),
            P("grp", "tp"),
            P("grp", "tp"),
            P("tp", "grp"),
            P("pool", "grp", "tp"),
            P("pool", "grp", "tp"),
            P("pool", "grp", "tp"),
            P("pool", "grp", "tp"),
            P("pool"),
            P("pool"),
            P("grp"),
            P("grp", ("pool", "tp")),
            P("grp", ("pool", "tp")),
            P(("pool", "tp"), "grp"),
        ),
        out_specs=P(("pool", "tp"), "grp"),
        check_vma=False,
    )
```

profile of v0, /device:TPU:1, one launch (start us, length us, event | category | flops | bytes accessed | tf_op | source)
XLA Modules:
  0.0 672.8 jit_solution(15598244335575411505)
XLA Ops:
  6.5 0.8 fusion.59
  7.4 0.7 broadcast_subtract_fusion
  8.1 1.6 multiply_reduce_fusion
  9.7 9.5 %psum.56 = f32[256]{0:T(256)S(1)} all-reduce(f32[256]{0:T(256)S(1)} %multiply_reduce_fusion), channel_id=1, replica_groups=mesh['pool'=4,'grp'=4,'tp'=8] {'grp'}, use_global_device_ids=true, to_apply=%region_1.0 | all-reduce | flops 256 | bytes 2048 | tf_op jit(solution)/shard_map/psum | solution.py:53
  19.2 4.9 fusion.46
  24.1 0.5 fusion.45
  24.7 0.5 fusion.44
  25.2 26.5 %all-reduce.9 = (bf16[256,1024]{1,0:T(8,128)(2,1)S(1)}, bf16[256,128]{1,0:T(8,128)(2,1)S(1)}, bf16[256,128]{1,0:T(8,128)(2,1)S(1)}) all-reduce(f32[256,1024]{1,0:T(8,128)} %fusion.46, f32[256,128]{1,0:T(8,128)S(1)} %fusion.45, f32[256,128]{1,0:T(8,128)S(1)} %fusion.44), channel_id=1, replica_groups=mesh['pool'=4,'grp'=4,'tp'=8] {'grp'}, use_global_device_ids=true, to_apply=%region_2.0 | all-reduce | flops 327680 | bytes 1966080 | tf_op jit(solution)/shard_map/psum | solution.py:59
  51.8 0.6 reduce-window.6
  52.4 0.2 slice_reduce_fusion
  52.6 0.2 reduce-window.9
  53.0 1.6 scatter_custom_fusion
  54.6 0.8 gather_fusion
  55.4 13.1 %bitcast_reduce_fusion = (f32[2,128,8]{1,2,0:T(8,128)S(1)}, f32[2,128,8,4096]{3,1,2,0:T(8,128)}) fusion(bf16[2,4096,128]{2,1,0:T(8,128)(2,1)S(1)} %copy-done, bf16[2,128,8,128]{3,2,1,0:T(8,128)(2,1)S(1)} %bitcast.165), kind=kOutput, calls=%fused_computation.17 | convolution fusion | flops 2164258816 | bytes 36184064 | tf_op jit(solution)/shard_map/pskgd,pjkd->pskgj/dot_general | solution.py:89
  68.6 0.7 gather_fusion.1
  69.5 4.5 fusion.47
  74.1 0.7 gather_fusion.2
  74.9 13.8 %fusion.17 = f32[2,128,1,8,128]{4,1,3,0,2:T(8,128)S(1)} fusion(bf16[2,4096,128]{2,1,0:T(8,128)(2,1)} %param.25, f32[2,128,8]{1,2,0:T(8,128)S(1)} %copy.48, f32[2,128,8,4096]{3,1,2,0:T(8,128)} %get-tuple-element.234), kind=kOutput, calls=%fused_computation.37 | convolution fusion | flops 2172649472 | bytes 36708352 | tf_op jit(solution)/shard_map/pskgj,pjkd->pskgd/dot_general | solution.py:105
  88.7 1.6 copy.50
  90.3 2.9 gather_fusion.4
  93.2 4.7 convolution_add_fusion
  98.0 10.4 %all-gather.1 = f32[1024,8]{1,0:T(8,128)S(1)} all-gather(f32[256,8]{1,0:T(8,128)S(1)} %max.43), channel_id=3, replica_groups=mesh['pool'=4,'grp'=4,'tp'=8] {'grp'}, dimensions={0}, use_global_device_ids=true | all-gather | bytes 40960 | tf_op jit(solution)/shard_map/all_gather | solution.py:13
  108.5 14.6 %convert_reduce_fusion = f32[2,128,8]{1,2,0:T(8,128)S(1)} fusion(f32[2,128,8]{1,2,0:T(8,128)S(1)} %copy.48, f32[2,128,8,4096]{3,1,2,0:T(8,128)} %get-tuple-element.234), kind=kLoop, calls=%fused_computation.20 | loop fusion | flops 41940992 | bytes 33570816 | tf_op jit(solution)/shard_map/reduce_sum | solution.py:103
  123.3 0.7 gather_fusion.3
  124.0 0.7 convert_reduce_fusion.1
  124.8 14.8 %all-gather.2 = f32[1024,8]{1,0:T(8,128)S(1)} all-gather(f32[256,8]{1,0:T(8,128)S(1)} %add.162), channel_id=4, replica_groups=mesh['pool'=4,'grp'=4,'tp'=8] {'grp'}, dimensions={0}, use_global_device_ids=true | all-gather | bytes 40960 | tf_op jit(solution)/shard_map/all_gather | solution.py:13
  139.7 0.2 copy.54
  140.0 0.4 fusion.32
  140.5 16.9 %all-gather.8.cloned.1.call-done = f32[1024,8,128]{2,1,0:T(8,128)} async-done(((f32[256,8,128]{2,1,0:T(8,128)}), f32[1024,8,128]{2,1,0:T(8,128)}) %all-gather.8.cloned.1.call-update) | async-done | bytes 4194320 | tf_op jit(solution)/shard_map/all_gather | solution.py:13
  157.4 1.3 slice_bitcast_fusion
  158.7 6.7 while.19
  159.0 1.9 fusion.65
  161.3 1.9 fusion.65
  163.5 1.9 fusion.65
  165.8 1.0 divide_convert_fusion
  166.9 4.8 fusion.28
  171.8 1.6 convert_element_type.68
  173.4 103.1 %all-reduce.6.cloned.1.call-done = f32[256,2048]{1,0:T(8,128)} async-done(((f32[256,2048]{1,0:T(8,128)}), f32[256,2048]{1,0:T(8,128)}) %all-reduce.6.cloned.1.call-update) | async-done | bytes 2097168 | tf_op jit(solution)/shard_map/psum | solution.py:136
  276.5 1.7 add_convert_fusion.1
  278.2 85.9 %all-gather.6.cloned.1.call-done = bf16[1024,2048]{1,0:T(8,128)(2,1)} async-done(((bf16[32,2048]{1,0:T(8,128)(2,1)}), bf16[1024,2048]{1,0:T(8,128)(2,1)}) %all-gather.6.cloned.1.call-update) | async-done | bytes 4194320 | tf_op jit(solution)/shard_map/all_gather | solution.py:140
  364.2 3.1 fusion.9
  367.2 8.5 %psum.61 = f32[1024]{0:T(1024)S(1)} all-reduce(f32[1024]{0:T(1024)S(1)} %fusion.9), channel_id=1, replica_groups=mesh['pool'=4,'grp'=4,'tp'=8] {'grp'}, use_global_device_ids=true, to_apply=%region_17.18 | all-reduce | flops 1024 | bytes 8192 | tf_op jit(solution)/shard_map/psum | solution.py:142
  375.7 6.4 fusion.22
  382.1 3.5 fusion.24
  385.6 85.0 %all-reduce.8.cloned.1.call-done = (f32[1024,448]{0,1:T(8,128)}, f32[1024,448]{0,1:T(8,128)}) async-done(((f32[1024,448]{0,1:T(8,128)}, f32[1024,448]{0,1:T(8,128)}), (f32[1024,448]{0,1:T(8,128)}, f32[1024,448]{0,1:T(8,128)})) %all-reduce.8.cloned.1.call-update) | async-done | bytes 3670032 | tf_op jit(solution)/shard_map/psum | solution.py:147
  470.7 8.3 %fusion.26 = f32[1024,2048]{1,0:T(8,128)} fusion(bf16[448,2048]{1,0:T(8,128)(2,1)} %param.33, f32[1024,448]{0,1:T(8,128)} %get-tuple-element.224, f32[1024,448]{0,1:T(8,128)} %get-tuple-element.225), kind=kOutput, calls=%fused_computation.44 | convolution fusion | flops 1881800704 | bytes 13893632 | tf_op jit(solution)/shard_map/dot_general | solution.py:150
  478.9 185.7 %reduce-scatter.2.cloned.1.call-done = f32[32,2048]{1,0:T(8,128)} async-done(((f32[1024,2048]{1,0:T(8,128)}), f32[32,2048]{1,0:T(8,128)}) %reduce-scatter.2.cloned.1.call-update) | async-done | bytes 262160 | tf_op jit(solution)/shard_map/reduce_scatter | solution.py:149
  664.6 1.6 add_convert_fusion
  (80 shorter events, 2.6 us)
Async XLA Ops:
  6.5 48.9 %copy-start = (bf16[2,4096,128]{2,1,0:T(8,128)(2,1)S(1)}, bf16[2,4096,128]{2,1,0:T(8,128)(2,1)}, u32[]{:S(2)}) copy-start(bf16[2,4096,128]{2,1,0:T(8,128)(2,1)} %param.24) | copy-start | bytes 6291460
  6.5 150.9 %all-gather.8.cloned.1.call-start = ((), (), s32[]{:S(2)}) async-start(), calls=%async_computation.4 | async-start | bytes 5242880 | tf_op jit(solution)/shard_map/all_gather | solution.py:13
  8.1 16.1 %copy-start.2 = (bf16[256,2048]{1,0:T(8,128)(2,1)S(1)}, bf16[256,2048]{1,0:T(8,128)(2,1)}, u32[]{:S(2)}) copy-start(bf16[256,2048]{1,0:T(8,128)(2,1)} %param.18) | copy-start | bytes 3145732
  8.1 16.1 %copy-start.11 = (f32[2048]{0:T(1024)S(1)}, f32[2048]{0:T(1024)}, u32[]{:S(2)}) copy-start(f32[2048]{0:T(1024)} %param.19) | copy-start | bytes 24580
  19.2 4.9 copy-start.9
  19.2 5.4 copy-start.10
  24.1 28.8 %copy-start.6 = (s32[256]{0:T(256)S(1)}, s32[256]{0:T(256)}, u32[]{:S(2)}) copy-start(s32[256]{0:T(256)} %param.28) | copy-start | bytes 3076
  55.4 14.0 %copy-start.7 = (s32[256]{0:T(256)S(1)}, s32[256]{0:T(256)}, u32[]{:S(2)}) copy-start(s32[256]{0:T(256)} %param.29) | copy-start | bytes 3076
  98.0 178.5 %all-reduce.6.cloned.1.call-start = ((), (), s32[]{:S(2)}) async-start(), calls=%async_computation.1 | async-start | bytes 4194304 | tf_op jit(solution)/shard_map/psum | solution.py:136
  166.8 4.9 copy-start.3
  171.7 204.0 %copy-start.12 = (f32[2048]{0:T(1024)S(1)}, f32[2048]{0:T(1024)}, u32[]{:S(2)}) copy-start(f32[2048]{0:T(1024)} %param.30) | copy-start | bytes 24580
  171.7 192.4 %all-gather.6.cloned.1.call-start = ((), (), s32[]{:S(2)}) async-start(), calls=%async_computation.2 | async-start | bytes 4325376 | tf_op jit(solution)/shard_map/all_gather | solution.py:140
  278.2 192.5 %all-reduce.8.cloned.1.call-start = ((), (), s32[]{:S(2)}) async-start(), calls=%async_computation.5 | async-start | bytes 7340032 | tf_op jit(solution)/shard_map/psum | solution.py:147
  375.7 6.4 copy-start.4
  375.7 6.4 copy-start.8
  385.6 279.0 %reduce-scatter.2.cloned.1.call-start = ((), (), s32[]{:S(2)}) async-start(), calls=%async_computation.3 | async-start | bytes 8650752 | tf_op jit(solution)/shard_map/reduce_scatter | solution.py:149
  478.9 187.3 %copy-start.1 = (bf16[2,4096,128]{2,1,0:T(8,128)(2,1)S(1)}, bf16[2,4096,128]{2,1,0:T(8,128)(2,1)}, u32[]{:S(2)}) copy-start(bf16[2,4096,128]{2,1,0:T(8,128)(2,1)} %param.24) | copy-start | bytes 6291460
  478.9 185.7 %copy-start.5 = (bf16[32,2048]{1,0:T(8,128)(2,1)S(1)}, bf16[32,2048]{1,0:T(8,128)(2,1)}, u32[]{:S(2)}) copy-start(bf16[32,2048]{1,0:T(8,128)(2,1)} %add_convert_fusion.1) | copy-start | bytes 393220
Sparse Core Ops, SparseCore 0:
  98.1 59.2 all-gather.7
  171.8 104.5 all-reduce.5
  278.3 85.8 all-gather.5
  385.7 84.8 all-reduce.7
  479.1 185.5 reduce-scatter.1
where the time goes:
time: 673 us
  waiting for transfers between devices  477 us (71%)
  blocking collectives  69.7 us (10%)
  matrix products  65.4 us (10%)
  other arithmetic  34.3 us (5%)
  between operations  13.5 us (2%)
  local copies, waits for them, and re-layouts  12.8 us (2%)
    reduce_scatter x1, waiting for transfers between devices, body(): lax.psum_scatter(jnp.dot(act, w_down, preferred_element_type=jnp.float32)...  186 us
    psum x1, waiting for transfers between devices, body(): summed = lax.psum(partial_out, 'tp')  103 us
    all_gather x1, waiting for transfers between devices, body(): gathered = lax.all_gather(middle, ('pool', 'tp'), axis=0, tiled=True)  85.9 us
    psum x1, waiting for transfers between devices, body(): gate, upward = lax.psum((part_gate, part_upward), 'grp')  85 us
    psum x1, blocking collectives, body(): lax.psum((part_query, part_key, part_value), 'grp')  26.5 us
    all_gather x2, blocking collectives, joined(): everything = jax.tree.map(lambda part: lax.all_gather(part, axis), array)  25.2 us
    all_gather x1, waiting for transfers between devices, joined(): everything = jax.tree.map(lambda part: lax.all_gather(part, axis), array)  16.9 us
    reduce_sum x1, other arithmetic, body(): pre_weights.astype(jnp.float32).sum(axis=4)  14.6 us
  transfers between devices with their start and end apart: 5, of which 5 were waited for; matrix products, arithmetic and copies ran while one was open for 3% of the time, Pallas kernels for 0%

commit v1 on v0

--- a/solution.py
+++ b/solution.py
@@ -137,7 +137,8 @@
     summed = lax.dynamic_slice_in_dim(summed, tp_start, share, 0)
     own_hidden = lax.dynamic_slice_in_dim(hidden_float, tp_start, share, 0)
     middle = (own_hidden + summed).astype(jnp.bfloat16)
-    gathered = lax.all_gather(middle, ("pool", "tp"), axis=0, tiled=True)
+    sent = jnp.stack([middle] * lax.axis_size(("pool", "tp")))
+    gathered = jnp.concatenate(lax.all_to_all(sent, ("pool", "tp"), 0, 0), axis=0)
     gathered_float = gathered.astype(jnp.float32)
     ffn_squares = lax.psum(jnp.sum(gathered_float * gathered_float, axis=1), "grp")
     ffn_inverse = lax.rsqrt(ffn_squares / D + epsilon)

time: 673 us -> 640 us (0.951)
  waiting for transfers between devices: 477 us -> 388 us
  blocking collectives: 69.7 us -> 125 us
    all_gather x1 -> x0, waiting for transfers between devices: 85.9 us -> none  [body(): gathered = lax.all_gather(middle, ('pool', 'tp'), axis=0, tiled=True)]
    all_to_all x0 -> x1, blocking collectives: none -> 55.8 us  [body(): lax.all_to_all(sent, ('pool', 'tp'), 0, 0)]
  transfers between devices with their start and end apart: 5 -> 4, of which waited for: 5 -> 4; matrix products, arithmetic and copies ran while one was open for 3% -> 3% of each run, Pallas kernels for 0% -> 0%
where the time goes in v1:
time: 640 us
  waiting for transfers between devices  388 us (61%)
  blocking collectives  125 us (20%)
  matrix products  61.8 us (10%)
  other arithmetic  34.9 us (5%)
  local copies, waits for them, and re-layouts  15.3 us (2%)
  between operations  13.5 us (2%)
    reduce_scatter x1, waiting for transfers between devices, body(): lax.psum_scatter(jnp.dot(act, w_down, preferred_element_type=jnp.float32)...  186 us
    psum x1, waiting for transfers between devices, body(): summed = lax.psum(partial_out, 'tp')  103 us
    psum x1, waiting for transfers between devices, body(): gate, upward = lax.psum((part_gate, part_upward), 'grp')  82.5 us
    all_to_all x1, blocking collectives, body(): lax.all_to_all(sent, ('pool', 'tp'), 0, 0)  55.8 us
    psum x1, blocking collectives, body(): lax.psum((part_query, part_key, part_value), 'grp')  26.5 us
    all_gather x2, blocking collectives, joined(): everything = jax.tree.map(lambda part: lax.all_gather(part, axis), array)  25.2 us
    all_gather x1, waiting for transfers between devices, joined(): everything = jax.tree.map(lambda part: lax.all_gather(part, axis), array)  16.9 us
    reduce_sum x1, other arithmetic, body(): pre_weights.astype(jnp.float32).sum(axis=4)  14.6 us
  transfers between devices with their start and end apart: 4, of which 4 were waited for; matrix products, arithmetic and copies ran while one was open for 3% of the time, Pallas kernels for 0%

profile of v1, /device:TPU:1, one launch (start us, length us, event | category | flops | bytes accessed | tf_op | source)
XLA Modules:
  0.0 639.7 jit_solution(17779373161029489101)
XLA Ops:
  6.5 0.8 fusion.58
  7.4 0.7 broadcast_subtract_fusion
  8.1 1.6 multiply_reduce_fusion.1
  9.7 9.5 %psum.56 = f32[256]{0:T(256)S(1)} all-reduce(f32[256]{0:T(256)S(1)} %multiply_reduce_fusion.1), channel_id=1, replica_groups=mesh['pool'=4,'grp'=4,'tp'=8] {'grp'}, use_global_device_ids=true, to_apply=%region_1.0 | all-reduce | flops 256 | bytes 2048 | tf_op jit(solution)/shard_map/psum | solution.py:53
  19.2 4.9 fusion.41
  24.1 0.5 fusion.40
  24.7 0.5 fusion.39
  25.2 26.5 %all-reduce.9 = (bf16[256,1024]{1,0:T(8,128)(2,1)S(1)}, bf16[256,128]{1,0:T(8,128)(2,1)S(1)}, bf16[256,128]{1,0:T(8,128)(2,1)S(1)}) all-reduce(f32[256,1024]{1,0:T(8,128)} %fusion.41, f32[256,128]{1,0:T(8,128)S(1)} %fusion.40, f32[256,128]{1,0:T(8,128)S(1)} %fusion.39), channel_id=1, replica_groups=mesh['pool'=4,'grp'=4,'tp'=8] {'grp'}, use_global_device_ids=true, to_apply=%region_2.0 | all-reduce | flops 327680 | bytes 1966080 | tf_op jit(solution)/shard_map/psum | solution.py:59
  51.8 0.6 reduce-window.6
  53.0 1.6 scatter_custom_fusion
  54.6 0.8 gather_fusion
  55.4 13.1 %bitcast_reduce_fusion = (f32[2,128,8]{1,2,0:T(8,128)S(1)}, f32[2,128,8,4096]{3,1,2,0:T(8,128)}) fusion(bf16[2,4096,128]{2,1,0:T(8,128)(2,1)S(1)} %copy-done, bf16[2,128,8,128]{3,2,1,0:T(8,128)(2,1)S(1)} %bitcast.173), kind=kOutput, calls=%fused_computation.17 | convolution fusion | flops 2164258816 | bytes 36184064 | tf_op jit(solution)/shard_map/pskgd,pjkd->pskgj/dot_general | solution.py:89
  68.6 0.7 gather_fusion.1
  69.5 4.5 fusion.42
  74.1 0.7 gather_fusion.2
  74.9 13.8 %fusion.16 = f32[2,128,1,8,128]{4,1,3,0,2:T(8,128)S(1)} fusion(bf16[2,4096,128]{2,1,0:T(8,128)(2,1)} %param.25, f32[2,128,8]{1,2,0:T(8,128)S(1)} %copy.64, f32[2,128,8,4096]{3,1,2,0:T(8,128)} %get-tuple-element.241), kind=kOutput, calls=%fused_computation.36 | convolution fusion | flops 2172649472 | bytes 36708352 | tf_op jit(solution)/shard_map/pskgj,pjkd->pskgd/dot_general | solution.py:105
  88.7 1.6 copy.66
  90.3 2.9 gather_fusion.4
  93.2 4.7 convolution_add_fusion
  98.0 10.4 %all-gather.1 = f32[1024,8]{1,0:T(8,128)S(1)} all-gather(f32[256,8]{1,0:T(8,128)S(1)} %max.43), channel_id=3, replica_groups=mesh['pool'=4,'grp'=4,'tp'=8] {'grp'}, dimensions={0}, use_global_device_ids=true | all-gather | bytes 40960 | tf_op jit(solution)/shard_map/all_gather | solution.py:13
  108.5 14.6 %convert_reduce_fusion = f32[2,128,8]{1,2,0:T(8,128)S(1)} fusion(f32[2,128,8]{1,2,0:T(8,128)S(1)} %copy.64, f32[2,128,8,4096]{3,1,2,0:T(8,128)} %get-tuple-element.241), kind=kLoop, calls=%fused_computation.20 | loop fusion | flops 41940992 | bytes 33570816 | tf_op jit(solution)/shard_map/reduce_sum | solution.py:103
  123.3 0.7 gather_fusion.3
  124.0 0.7 convert_reduce_fusion.1
  124.8 14.8 %all-gather.2 = f32[1024,8]{1,0:T(8,128)S(1)} all-gather(f32[256,8]{1,0:T(8,128)S(1)} %add.162), channel_id=4, replica_groups=mesh['pool'=4,'grp'=4,'tp'=8] {'grp'}, dimensions={0}, use_global_device_ids=true | all-gather | bytes 40960 | tf_op jit(solution)/shard_map/all_gather | solution.py:13
  140.0 0.4 fusion.27
  140.5 16.9 %all-gather.5.cloned.1.call-done = f32[1024,8,128]{2,1,0:T(8,128)} async-done(((f32[256,8,128]{2,1,0:T(8,128)}), f32[1024,8,128]{2,1,0:T(8,128)}) %all-gather.5.cloned.1.call-update) | async-done | bytes 4194320 | tf_op jit(solution)/shard_map/all_gather | solution.py:13
  157.4 1.3 slice_bitcast_fusion
  158.7 6.7 %while.19 = (s32[]{:T(128)}, f32[256,1,8]{0,2,1:T(8,128)S(1)}, f32[256,1,8]{0,2,1:T(8,128)S(1)}, f32[256,1,8,128]{3,2,1,0:T(8,128)S(1)}, f32[4,256,1,8]{1,3,2,0:...) while((s32[]{:T(128)}, f32[256,1,8]{0,2,1:T(8,128)S(1)}, ...), condition=%wide.region_12.13_spmd, body=%wide.region_11.12_spmd.sunk | while | flops 800773 | bytes 3301531 | solution.py:19
  159.0 1.9 fusion.64
  161.3 1.9 fusion.64
  163.5 1.9 fusion.64
  165.8 1.0 divide_convert_fusion
  166.9 4.8 fusion.23
  171.8 1.6 convert_element_type.74
  173.3 103.1 %all-reduce.6.cloned.1.call-done = f32[256,2048]{1,0:T(8,128)} async-done(((f32[256,2048]{1,0:T(8,128)}), f32[256,2048]{1,0:T(8,128)}) %all-reduce.6.cloned.1.call-update) | async-done | bytes 2097168 | tf_op jit(solution)/shard_map/psum | solution.py:136
  276.5 1.1 add_convert_fusion.1
  277.5 0.5 stack.2
  278.0 55.8 %all_to_all.5 = bf16[32,32,2048]{2,1,0:T(8,128)(2,1)S(1)} all-to-all(bf16[32,32,2048]{2,1,0:T(8,128)(2,1)S(1)} %stack.2), channel_id=1, replica_groups=mesh['pool'=4,'grp'=4,'tp'=8] {'pool','tp'}, dimensions={0} | all-to-all | bytes 8388608 | tf_op jit(solution)/shard_map/all_to_all | solution.py:141
  333.8 1.9 copy-done.2
  335.7 0.9 multiply_reduce_fusion
  336.7 8.4 %psum.61 = f32[1024]{0:T(1024)S(1)} all-reduce(f32[1024]{0:T(1024)S(1)} %reduce_sum.55), channel_id=1, replica_groups=mesh['pool'=4,'grp'=4,'tp'=8] {'grp'}, use_global_device_ids=true, to_apply=%region_17.18 | all-reduce | flops 1024 | bytes 8192 | tf_op jit(solution)/shard_map/psum | solution.py:143
  345.1 3.3 fusion.10
  348.5 3.4 fusion.44
  351.9 3.4 fusion.43
  355.6 82.5 %all-reduce.8.cloned.1.call-done = (f32[1024,448]{0,1:T(8,128)}, f32[1024,448]{0,1:T(8,128)}) async-done(((f32[1024,448]{0,1:T(8,128)}, f32[1024,448]{0,1:T(8,128)}), (f32[1024,448]{0,1:T(8,128)}, f32[1024,448]{0,1:T(8,128)})) %all-reduce.8.cloned.1.call-update) | async-done | bytes 3670032 | tf_op jit(solution)/shard_map/psum | solution.py:148
  438.1 7.7 %fusion.21 = f32[1024,2048]{1,0:T(8,128)} fusion(bf16[448,2048]{1,0:T(8,128)(2,1)S(1)} %copy-done.10, f32[1024,448]{0,1:T(8,128)} %get-tuple-element.231, f32[1024,448]{0,1:T(8,128)} %get-tuple-element.232), kind=kOutput, calls=%fused_computation.41 | convolution fusion | flops 1881800704 | bytes 13893632 | tf_op jit(solution)/shard_map/dot_general | solution.py:151
  445.9 185.7 %reduce-scatter.2.cloned.1.call-done = f32[32,2048]{1,0:T(8,128)} async-done(((f32[1024,2048]{1,0:T(8,128)}), f32[32,2048]{1,0:T(8,128)}) %reduce-scatter.2.cloned.1.call-update) | async-done | bytes 262160 | tf_op jit(solution)/shard_map/reduce_scatter | solution.py:150
  631.5 1.6 add_convert_fusion
  (83 shorter events, 3.5 us)
Async XLA Ops:
  6.5 48.9 %copy-start = (bf16[2,4096,128]{2,1,0:T(8,128)(2,1)S(1)}, bf16[2,4096,128]{2,1,0:T(8,128)(2,1)}, u32[]{:S(2)}) copy-start(bf16[2,4096,128]{2,1,0:T(8,128)(2,1)} %param.24) | copy-start | bytes 6291460
  6.5 150.9 %all-gather.5.cloned.1.call-start = ((), (), s32[]{:S(2)}) async-start(), calls=%async_computation.4 | async-start | bytes 5242880 | tf_op jit(solution)/shard_map/all_gather | solution.py:13
  8.1 16.1 %copy-start.3 = (bf16[256,2048]{1,0:T(8,128)(2,1)S(1)}, bf16[256,2048]{1,0:T(8,128)(2,1)}, u32[]{:S(2)}) copy-start(bf16[256,2048]{1,0:T(8,128)(2,1)} %param.18) | copy-start | bytes 3145732
  8.1 16.1 %copy-start.13 = (f32[2048]{0:T(1024)S(1)}, f32[2048]{0:T(1024)}, u32[]{:S(2)}) copy-start(f32[2048]{0:T(1024)} %param.19) | copy-start | bytes 24580
  19.2 4.9 copy-start.11
  19.2 5.4 copy-start.12
  24.1 28.8 %copy-start.5 = (s32[256]{0:T(256)S(1)}, s32[256]{0:T(256)}, u32[]{:S(2)}) copy-start(s32[256]{0:T(256)} %param.28) | copy-start | bytes 3076
  55.4 14.0 %copy-start.7 = (s32[256]{0:T(256)S(1)}, s32[256]{0:T(256)}, u32[]{:S(2)}) copy-start(s32[256]{0:T(256)} %param.29) | copy-start | bytes 3076
  98.0 178.5 %all-reduce.6.cloned.1.call-start = ((), (), s32[]{:S(2)}) async-start(), calls=%async_computation.2 | async-start | bytes 4194304 | tf_op jit(solution)/shard_map/psum | solution.py:136
  166.8 4.9 copy-start.4
  171.7 266.4 %all-reduce.8.cloned.1.call-start = ((), (), s32[]{:S(2)}) async-start(), calls=%async_computation.5 | async-start | bytes 7340032 | tf_op jit(solution)/shard_map/psum | solution.py:148
  333.8 1.9 copy-start.2
  335.7 9.4 %copy-start.6 = (f32[2048]{0:T(1024)S(1)}, f32[2048]{0:T(1024)}, u32[]{:S(2)}) copy-start(f32[2048]{0:T(1024)} %param.30) | copy-start | bytes 24580
  345.1 3.4 copy-start.8
  348.5 3.4 copy-start.9
  351.9 86.3 %copy-start.10 = (bf16[448,2048]{1,0:T(8,128)(2,1)S(1)}, bf16[448,2048]{1,0:T(8,128)(2,1)}, u32[]{:S(2)}) copy-start(bf16[448,2048]{1,0:T(8,128)(2,1)} %param.33) | copy-start | bytes 5505028
  355.3 276.2 %reduce-scatter.2.cloned.1.call-start = ((), (), s32[]{:S(2)}) async-start(), calls=%async_computation.3 | async-start | bytes 8650752 | tf_op jit(solution)/shard_map/reduce_scatter | solution.py:150
  445.8 187.3 %copy-start.1 = (bf16[2,4096,128]{2,1,0:T(8,128)(2,1)S(1)}, bf16[2,4096,128]{2,1,0:T(8,128)(2,1)}, u32[]{:S(2)}) copy-start(bf16[2,4096,128]{2,1,0:T(8,128)(2,1)} %param.24) | copy-start | bytes 6291460
Sparse Core Ops, SparseCore 0:
  98.1 59.2 all-gather.4
  171.8 104.5 all-reduce.5
  355.4 82.6 all-reduce.7
  446.0 185.5 reduce-scatter.1
